TPU v7x, 256 devices: a whole 4x4x8 slice. The times are simulated.
256 devices in a mesh: gx: 16 (over x, y), gy: 16 (over z, core).
Axes of the slice: x: 4, y: 4, z: 8, core: 2. Of those that a mesh axis runs over, the one named last changes fastest.
Arguments:
- inv_factors: float32 [64, 64, 4096], P('gx', 'gy'), as said below
- couplings: float32 [64, 64, 2, 4096], P('gx', 'gy'), may hold values from -1.5 to 1.5
- stencil: int32 [64, 64, 2], P('gx', 'gy'), may hold values from 0 to 1
- coarse: int32 [64, 64], P('gx', 'gy'), may hold values from 0 to 1, as said below
Outputs:
- strength: float32 [64, 64, 2], P('gx', 'gy')
- restriction: bfloat16 [3072, 14, 4096], P(('gx', 'gy'))
Inputs may be any that keep to these rules, and one draw needn't show every extreme that they name: Each block of inv_factors is lower triangular with diagonal entries between 0.5 and 1. Each tile of 4 x 4 elements has at most 12 coarse elements, and some tile has exactly 12.
All inputs are finite; a program needn't handle non-finite values.
Results may differ from a plain program's by a relative error of at most 0.001.
Values sent between devices are 32-bit elements; how exact they have to be, the bound alone decides.
No kernel may reach another device: no remote copies, remote signals or barrier semaphores. Data moves between devices by JAX's collectives and lax.ppermute only.
A program may use at most 64 MiB of HBM per device.

v0:
```python
import math

import jax
import jax.numpy as jnp
from jax import lax
from jax.experimental import pallas as pl
from jax.experimental.pallas import tpu as pltpu
from jax.sharding import PartitionSpec as P

CAP = 12
PREC = lax.Precision.HIGH


def matmul(left_block, right_block):
    return jnp.einsum("...ij,...jk->...ik", left_block, right_block, precision=PREC)


def left_gram(left_block, right_block):
    return jnp.einsum("...ji,...jk->...ik", left_block, right_block, precision=PREC)


def shift_pairs(count, step):
    return [(i, i + step) for i in range(count) if 0 <= i + step < count]


def corner_pairs(n_x, n_y, step_x, step_y):
    pairs = []
    for a in range(n_x):
        for b in range(n_y):
            if 0 <= a + step_x < n_x and 0 <= b + step_y < n_y:
                pairs.append((a * n_y + b, (a + step_x) * n_y + (b + step_y)))
    return pairs


def row_band(pieces):
    return jnp.concatenate(pieces, axis=1)


def padded(values, before_x, before_y):
    widths = [(1, 0) if before_x else (0, 1), (1, 0) if before_y else (0, 1)]
    widths += [(0, 0)] * (values.ndim - 2)
    return jnp.pad(values, widths)


def split(value):
    high = value.astype(jnp.bfloat16)
    low = (value - high.astype(jnp.float32)).astype(jnp.bfloat16)
    return high, low


def dot3(left, right, right_t=False):
    dims = (((1,), (1,)), ((), ())) if right_t else (((1,), (0,)), ((), ()))

    def one(a, b):
        return lax.dot_general(a, b, dims, preferred_element_type=jnp.float32)

    return one(left[0], right[0]) + one(left[0], right[1]) + one(left[1], right[0])


def local_kernel(side_ref, slot_ref, fine_ref, lead_ref, factor_ref, minus_ref,
                 xlo_ref, xhi_ref, ylo_ref, yhi_ref, cll_ref, clh_ref, chl_ref, chh_ref,
                 strong_ref, restrict_ref, pg, wg, gg, yg, zg):
    nx, ny = fine_ref.shape[0], fine_ref.shape[1]
    blk = fine_ref.shape[2:]
    zero = jnp.zeros(blk, jnp.float32)
    wide_x, wide_y = nx + 4, ny + 4
    pg_src, wg_src, gg_src = {}, {}, {}
    for i in range(nx):
        for j in range(ny):
            pg_src[(3 + i, 3 + j)] = (fine_ref, (i, j))
            gg_src[(1 + i, 1 + j)] = (factor_ref, (i, j))
            for e in range(2):
                wg_src[(2 + i, 2 + j, e)] = (lead_ref, (i, j, e))
    for c in range(ny):
        for r in range(3):
            pg_src[(r, 3 + c)] = (xlo_ref, (r * ny + c,))
            pg_src[(nx + 3 + r, 3 + c)] = (xhi_ref, (r * ny + c,))
        for r in range(2):
            for e in range(2):
                wg_src[(r, 2 + c, e)] = (xlo_ref, (3 * ny + (r * ny + c) * 2 + e,))
                wg_src[(nx + 2 + r, 2 + c, e)] = (xhi_ref, (3 * ny + (r * ny + c) * 2 + e,))
        gg_src[(0, 1 + c)] = (xlo_ref, (7 * ny + c,))
        gg_src[(nx + 1, 1 + c)] = (xhi_ref, (7 * ny + c,))
    for i in range(nx):
        for r in range(3):
            pg_src[(3 + i, r)] = (ylo_ref, (i * 3 + r,))
            pg_src[(3 + i, ny + 3 + r)] = (yhi_ref, (i * 3 + r,))
        for r in range(2):
            for e in range(2):
                wg_src[(2 + i, r, e)] = (ylo_ref, (3 * nx + (i * 2 + r) * 2 + e,))
                wg_src[(2 + i, ny + 2 + r, e)] = (yhi_ref, (3 * nx + (i * 2 + r) * 2 + e,))
        gg_src[(1 + i, 0)] = (ylo_ref, (7 * nx + i,))
        gg_src[(1 + i, ny + 1)] = (yhi_ref, (7 * nx + i,))
    for ref, px, py, wx, wy in ((cll_ref, 1, 1, 1, 1), (clh_ref, 1, ny + 3, 1, ny + 2),
                                (chl_ref, nx + 3, 1, nx + 2, 1),
                                (chh_ref, nx + 3, ny + 3, nx + 2, ny + 2)):
        for a in range(2):
            for b in range(2):
                pg_src[(px + a, py + b)] = (ref, (a * 2 + b,))
        for e in range(2):
            wg_src[(wx, wy, e)] = (ref, (4 + e,))

    def block(ref, at):
        if ref is None:
            return zero
        if len(at) == 1 and ref.shape[-1] == 2 * blk[-1]:
            half = at[0] % 2
            return ref[at[0] // 2, :, half * blk[-1] : (half + 1) * blk[-1]]
        return ref[at]

    for i in range(nx + 6):
        for j in range(ny + 6):
            pg[i, j] = block(*pg_src.get((i, j), (None, None)))
    for i in range(wide_x):
        for j in range(wide_y):
            for e in range(2):
                wg[i, j, e] = block(*wg_src.get((i, j, e), (None, None)))
    for i in range(nx + 2):
        for j in range(ny + 2):
            gg[i, j] = block(*gg_src.get((i, j), (None, None)))

    def side(i, j, d):
        return side_ref[(i * wide_y + j) * 2 + d]

    def outside(k, low, size):
        return max(low - k, k - (low + size - 1), 0)

    for i in range(wide_x):
        for j in range(wide_y):
            if outside(i, 2, nx) + outside(j, 2, ny) > 2:
                continue
            sx = side(i, j, 0)
            sy = side(i, j, 1)
            yg[i, j, 0] = dot3(split(wg[i, j, 0]), split(pg[i + 2 * sx, j + 1]))
            yg[i, j, 1] = dot3(split(wg[i, j, 1]), split(pg[i + 1, j + 2 * sy]))

    for i in range(nx + 2):
        for j in range(ny + 2):
            if outside(i, 1, nx) + outside(j, 1, ny) > 1:
                continue
            zg[i, j, 0] = pg[i + 2, j + 2]
            for e in range(2):
                s = side(i + 1, j + 1, e)
                ui = i + 2 * s if e == 0 else i + 1
                uj = j + 1 if e == 0 else j + 2 * s
                lead = split(wg[i + 1, j + 1, e])
                zg[i, j, 1 + 3 * e] = dot3(lead, split(pg[ui + 1, uj + 1]))
                zg[i, j, 2 + 3 * e] = dot3(lead, split(yg[ui, uj, 0]))
                zg[i, j, 3 + 3 * e] = dot3(lead, split(yg[ui, uj, 1]))

    def strong_step(p, carry):
        i = p // ny
        j = p % ny
        factor = split(factor_ref[i, j])
        for d in range(2):
            s = side(i + 2, j + 2, d)
            up = gg[i + 2 * s, j + 1] if d == 0 else gg[i + 1, j + 2 * s]
            scaled = dot3(split(dot3(factor, split(minus_ref[i, j, d]))), split(up), True)
            total = jnp.sum(scaled * scaled, axis=(0, 1), keepdims=True)
            strong_ref[p * 2 + d] = jnp.broadcast_to(total * (1.0 / scaled.size), (1, 128))
        return carry

    lax.fori_loop(0, nx * ny, strong_step, 0, unroll=True)

    def slot_step(s, carry):
        cell = slot_ref[s * 4]
        weight = slot_ref[s * 4 + 3].astype(jnp.float32)
        ci = cell // ny
        cj = cell % ny
        for d in range(2):
            n = slot_ref[s * 4 + 1 + d]
            ni = n // (ny + 2)
            nj = n % (ny + 2)
            coupling = split(minus_ref[ci, cj, d])
            for w in range(7):
                row = dot3(coupling, split(zg[ni, nj, w]))
                restrict_ref[s, d * 7 + w] = (row * weight).astype(restrict_ref.dtype)
        return carry

    lax.fori_loop(0, restrict_ref.shape[0], slot_step, 0, unroll=True)


def face_sources(nx, ny, side):
    sources = []
    if side in ("xhi", "xlo"):
        rows = {d: (range(nx - d, nx) if side == "xhi" else range(d)) for d in (1, 2, 3)}
        for r in rows[3]:
            for c in range(ny):
                sources.append(("fine", (r, c)))
        for r in rows[2]:
            for c in range(ny):
                for e in range(2):
                    sources.append(("lead", (r, c, e)))
        for r in rows[1]:
            for c in range(ny):
                sources.append(("factor", (r, c)))
        codes = [(r, c, e) for r in rows[2] for c in range(ny) for e in range(2)]
    else:
        cols = {d: (range(ny - d, ny) if side == "yhi" else range(d)) for d in (1, 2, 3)}
        for i in range(nx):
            for r in cols[3]:
                sources.append(("fine", (i, r)))
        for i in range(nx):
            for r in cols[2]:
                for e in range(2):
                    sources.append(("lead", (i, r, e)))
        for i in range(nx):
            for r in cols[1]:
                sources.append(("factor", (i, r)))
        codes = [(i, r, e) for i in range(nx) for r in cols[2] for e in range(2)]
    return sources, codes


def code_tile(side_ref, codes, ny, shape):
    rows = lax.broadcasted_iota(jnp.int32, shape, 0)
    lanes = lax.broadcasted_iota(jnp.int32, shape, 1)
    tile = jnp.zeros(shape, jnp.float32)
    for k, (i, j, e) in enumerate(codes):
        value = side_ref[(i * ny + j) * 2 + e].astype(jnp.float32)
        tile = jnp.where((rows == 0) & (lanes == k), value, tile)
    return tile


def pack_kernel(side_ref, fine_ref, lead_ref, factor_ref, *out_refs):
    nx, ny = fine_ref.shape[0], fine_ref.shape[1]
    width = fine_ref.shape[-1]
    named = {"fine": fine_ref, "lead": lead_ref, "factor": factor_ref}
    for out, side in zip(out_refs[:4], ("xhi", "xlo", "yhi", "ylo")):
        sources, codes = face_sources(nx, ny, side)
        for k, (name, at) in enumerate(sources):
            out[k // 2, :, (k % 2) * width : (k % 2 + 1) * width] = named[name][at]
        last = len(sources)
        out[last // 2] = code_tile(side_ref, codes, ny, out.shape[1:])
    for out, (sx, sy) in zip(out_refs[4:], ((1, 1), (1, -1), (-1, 1), (-1, -1))):
        rows2 = range(nx - 2, nx) if sx == 1 else range(2)
        cols2 = range(ny - 2, ny) if sy == 1 else range(2)
        row1 = nx - 1 if sx == 1 else 0
        col1 = ny - 1 if sy == 1 else 0
        blocks = [fine_ref[a, b] for a in rows2 for b in cols2]
        blocks += [lead_ref[row1, col1, e] for e in range(2)]
        for k, value in enumerate(blocks):
            out[k // 2, :, (k % 2) * width : (k % 2 + 1) * width] = value
        out[len(blocks) // 2] = code_tile(side_ref, [(row1, col1, 0), (row1, col1, 1)], ny,
                                          out.shape[1:])


def pack_buffers(stencil, fine_own, lead_own, factor_own):
    nx, ny = fine_own.shape[:2]
    blk = fine_own.shape[2:]
    face_count = len(face_sources(nx, ny, "xhi")[0]) + 1
    face_y_count = len(face_sources(nx, ny, "yhi")[0]) + 1
    vmem = pl.BlockSpec(memory_space=pltpu.VMEM)
    smem = pl.BlockSpec(memory_space=pltpu.SMEM)
    paired = lambda count: jax.ShapeDtypeStruct(((count + 1) // 2, blk[0], 2 * blk[1]), jnp.float32)
    shapes = [paired(face_count)] * 2 + [paired(face_y_count)] * 2
    shapes += [paired(7)] * 4
    return pl.pallas_call(
        pack_kernel,
        out_shape=tuple(shapes),
        in_specs=[smem, vmem, vmem, vmem],
        out_specs=tuple([vmem] * 8),
    )(stencil.reshape(-1), fine_own, lead_own, factor_own)


def local_compute(side_flat, slot_table, fine_own, lead_own, factor_own, minus_own, buffers):
    nx, ny = fine_own.shape[:2]
    blk = fine_own.shape[2:]
    vmem = pl.BlockSpec(memory_space=pltpu.VMEM)
    smem = pl.BlockSpec(memory_space=pltpu.SMEM)
    f32 = jnp.float32
    strong, restrict = pl.pallas_call(
        local_kernel,
        out_shape=(jax.ShapeDtypeStruct((nx * ny * 2, 1, 128), f32),
                   jax.ShapeDtypeStruct((CAP, 14) + blk, jnp.bfloat16)),
        in_specs=[smem, smem] + [vmem] * (4 + len(buffers)),
        out_specs=(vmem, vmem),
        scratch_shapes=[
            pltpu.VMEM((nx + 6, ny + 6) + blk, f32),
            pltpu.VMEM((nx + 4, ny + 4, 2) + blk, f32),
            pltpu.VMEM((nx + 2, ny + 2) + blk, f32),
            pltpu.VMEM((nx + 4, ny + 4, 2) + blk, f32),
            pltpu.VMEM((nx + 2, ny + 2, 7) + blk, f32),
        ],
        compiler_params=pltpu.CompilerParams(vmem_limit_bytes=60 * 1024 * 1024),
    )(side_flat, slot_table, fine_own, lead_own, factor_own, minus_own, *buffers)
    return strong[:, 0, 0].reshape(nx, ny, 2), restrict


def on_device(inv_factors, couplings, stencil, coarse):
    nx, ny, flat = inv_factors.shape
    order = math.isqrt(flat)
    blk = (order, order)
    n_gx = lax.axis_size("gx")
    n_gy = lax.axis_size("gy")
    total_x = nx * n_gx
    total_y = ny * n_gy
    coord_x = lax.axis_index("gx") * nx + jnp.arange(nx, dtype=jnp.int32)
    coord_y = lax.axis_index("gy") * ny + jnp.arange(ny, dtype=jnp.int32)
    target_x = coord_x[:, None] + 2 * stencil[:, :, 0] - 1
    target_y = coord_y[None, :] + 2 * stencil[:, :, 1] - 1
    reach = jnp.stack(
        [(target_x >= 0) & (target_x < total_x), (target_y >= 0) & (target_y < total_y)], axis=-1
    )
    minus_own = (couplings * (-reach.astype(jnp.float32))[:, :, :, None]).reshape(
        (nx, ny, 2) + blk
    )
    factor_own = inv_factors.reshape((nx, ny) + blk)
    fine_own = (1 - coarse).astype(jnp.float32)[:, :, None, None] * left_gram(
        factor_own, factor_own
    )
    lead_own = matmul(fine_own[:, :, None], minus_own)

    packed = pack_buffers(stencil, fine_own, lead_own, factor_own)
    from_xlo = lax.ppermute(packed[0], "gx", shift_pairs(n_gx, 1))
    from_xhi = lax.ppermute(packed[1], "gx", shift_pairs(n_gx, -1))
    from_ylo = lax.ppermute(packed[2], "gy", shift_pairs(n_gy, 1))
    from_yhi = lax.ppermute(packed[3], "gy", shift_pairs(n_gy, -1))
    corners = {}
    for step, buffer in zip(((1, 1), (1, -1), (-1, 1), (-1, -1)), packed[4:]):
        corners[step] = lax.ppermute(buffer, ("gx", "gy"),
                                     corner_pairs(n_gx, n_gy, *step))

    def face_codes(buffer, count, along_x):
        at = 3 * count + 2 * count * 2 + count
        codes = buffer[at // 2, 0, (at % 2) * order : (at % 2) * order + 2 * count * 2]
        codes = codes.astype(jnp.int32)
        return codes.reshape((2, count, 2) if along_x else (count, 2, 2))

    cxl = face_codes(from_xlo, ny, True)
    cxh = face_codes(from_xhi, ny, True)
    cyl = face_codes(from_ylo, nx, False)
    cyh = face_codes(from_yhi, nx, False)

    def unpack_corner(buffer):
        return (None, None, buffer[3, 0, 0:2].astype(jnp.int32).reshape(1, 1, 2))

    c_ll = unpack_corner(corners[(1, 1)])
    c_lh = unpack_corner(corners[(1, -1)])
    c_hl = unpack_corner(corners[(-1, 1)])
    c_hh = unpack_corner(corners[(-1, -1)])

    def cycle(k, lo_x, own, hi_x, lo_y, hi_y):
        return jnp.concatenate(
            [
                row_band([padded(c_ll[k], True, True), lo_x, padded(c_lh[k], True, False)]),
                row_band([lo_y, own, hi_y]),
                row_band([padded(c_hl[k], False, True), hi_x, padded(c_hh[k], False, False)]),
            ],
            axis=0,
        )

    side_cycle = cycle(2, cxl, stencil, cxh, cyl, cyh)

    cell_count = nx * ny
    flat_coarse = coarse.reshape(cell_count)
    slot_rank = jnp.cumsum(flat_coarse, dtype=jnp.int32) - flat_coarse
    chosen = (
        (slot_rank[None, :] == jnp.arange(CAP, dtype=jnp.int32)[:, None])
        & (flat_coarse[None, :] == 1)
    ).astype(jnp.int32)
    source = jnp.sum(
        chosen * jnp.arange(cell_count, dtype=jnp.int32)[None, :], axis=1, dtype=jnp.int32
    )
    filled = jnp.sum(chosen, axis=1, dtype=jnp.int32)
    span = ny + 2
    own_i = jnp.arange(nx, dtype=jnp.int32)[:, None] + 1
    own_j = jnp.arange(ny, dtype=jnp.int32)[None, :] + 1
    up_index = jnp.stack(
        [(own_i + 2 * stencil[:, :, 0] - 1) * span + own_j,
         own_i * span + own_j + 2 * stencil[:, :, 1] - 1],
        axis=-1,
    ).reshape(cell_count, 2)
    picked = jnp.take(up_index, source, axis=0, mode="clip")
    slot_table = jnp.concatenate([source[:, None], picked, filled[:, None]], axis=1).reshape(-1)
    buffers = (from_xlo, from_xhi, from_ylo, from_yhi, corners[(1, 1)], corners[(1, -1)],
               corners[(-1, 1)], corners[(-1, -1)])
    strong, restrict = local_compute(side_cycle.reshape(-1), slot_table, fine_own, lead_own,
                                     factor_own, minus_own, buffers)
    return (strong, restrict.reshape(CAP, 14, flat))


def solution(mesh):
    placed = (P("gx", "gy", None), P("gx", "gy", None, None), P("gx", "gy", None), P("gx", "gy"))
    return jax.shard_map(
        on_device,
        mesh=mesh,
        in_specs=placed,
        out_specs=(P("gx", "gy", None), P(("gx", "gy"), None, None)),
        check_vma=False,
    )
```

profile of v0, /device:TPU:121, one launch (start us, length us, event | category | flops | bytes accessed | tf_op | source)
XLA Modules:
  0.0 81.5 jit_solution(858522853368127322)
XLA Ops:
  0.6 0.7 subtract_convert_fusion
  1.3 0.8 copy.57
  2.1 0.8 %compare_and_fusion.1 = (pred[4,4,1]{1,2,0:T(4,128)(4,1)S(1)}, pred[4,4,1]{1,2,0:T(4,128)(4,1)S(1)}) fusion(s32[4]{0:T(128)S(1)} %get-tuple-element.37, s32[4,4,2]{1,2,0:T(2,128)} %param.6, s32[4]{0:T(128)S(1)} %get-tuple-element.36), kind=kLoop, calls=%fused_computation.19 | loop fusion | flops 192 | bytes 192 | tf_op jit(solution)/shard_map/and | solution.py:302
  3.0 0.1 copy.59
  3.1 0.6 reshape.190.side_ref
  3.7 1.2 %reshape.191.factor_ref = f32[4,4,64,64]{3,2,1,0:T(8,128)S(1)} reshape(f32[4,4,4096]{2,1,0:T(4,128)} %param.4) | data formatting | bytes 524288 | tf_op jit(solution)/shard_map/reshape | solution.py:307
  4.9 1.5 %broadcast_multiply_fusion = f32[4,4,2,4096]{3,2,1,0:T(2,128)S(1)} fusion(f32[4,4,2,4096]{3,2,1,0:T(2,128)} %param.5, f32[4,4,2]{2,1,0:T(4,128)S(1)} %copy.59), kind=kLoop, calls=%fused_computation.4 | loop fusion | flops 131072 | bytes 1048704 | tf_op jit(solution)/shard_map/mul | solution.py:304
  6.5 0.6 reshape.192.minus_ref
  7.1 0.6 convolution_multiply_fusion.fine_ref
  7.7 0.0 copy-start.2
  7.7 0.0 copy-start.12
  7.7 0.0 copy-start.11
  7.7 1.5 %convolution_bitcast_fusion.lead_ref = f32[4,4,2,64,64]{4,3,2,1,0:T(8,128)} fusion(f32[4,4,2,64,64]{4,3,2,1,0:T(8,128)S(1)} %reshape.192.minus_ref, f32[4,4,64,64]{3,2,1,0:T(8,128)S(1)} %convolution_multiply_fusion.fine_ref), kind=kOutput, calls=%fused_computation.1 | convolution fusion | flops 50331648 | bytes 1310720 | tf_op jit(solution)/shard_map/...ij,...jk->...ik/dot_general | solution.py:15
  9.3 0.0 copy-done.2
  9.3 3.7 %shard_map.59 = (f32[17,64,128]{2,1,0:T(8,128)}, f32[17,64,128]{2,1,0:T(8,128)}, f32[17,64,128]{2,1,0:T(8,128)}, f32[17,64,128]{2,1,0:T(8,128)}, f32[4,64,128]{2...) custom-call(s32[32]{0:T(128)} %reshape.190.side_ref, ...), custom_call_target="tpu_custom_call" | custom-call | tf_op jit(solution)/shard_map/pallas_call | solution.py:257
  12.9 5.9 %collective-permute-start = (f32[4,64,128]{2,1,0:T(8,128)}, f32[4,64,128]{2,1,0:T(8,128)S(1)}, u32[]{:S(2)}, u32[]{:S(2)}) collective-permute-start(f32[4,64,128]{2,1,0:T(8,128)} %get-tuple-element.12), channel_id=1, source_target_pairs={{0,17},{1,18},{2,19},{3,20},{4,21},{5,22},{6,23},{7,24},{8,25},{9,... | collective-permute-start | bytes 393224 | tf_op jit(solution)/shard_map/ppermute | solution.py:320
  18.8 1.9 %collective-permute-start.2 = (f32[4,64,128]{2,1,0:T(8,128)}, f32[4,64,128]{2,1,0:T(8,128)S(1)}, u32[]{:S(2)}, u32[]{:S(2)}) collective-permute-start(f32[4,64,128]{2,1,0:T(8,128)} %get-tuple-element.14), channel_id=1, source_target_pairs={{1,16},{2,17},{3,18},{4,19},{5,20},{6,21},{7,22},{8,23},{9,24},{10... | collective-permute-start | bytes 393224 | tf_op jit(solution)/shard_map/ppermute | solution.py:320
  20.8 5.8 %collective-permute-start.5 = (f32[4,64,128]{2,1,0:T(8,128)}, f32[4,64,128]{2,1,0:T(8,128)S(1)}, u32[]{:S(2)}, u32[]{:S(2)}) collective-permute-start(f32[4,64,128]{2,1,0:T(8,128)} %get-tuple-element.17), channel_id=1, source_target_pairs={{16,1},{17,2},{18,3},{19,4},{20,5},{21,6},{22,7},{23,8},{24,9},{25... | collective-permute-start | bytes 393224 | tf_op jit(solution)/shard_map/ppermute | solution.py:320
  26.5 1.9 %collective-permute-start.7 = (f32[4,64,128]{2,1,0:T(8,128)}, f32[4,64,128]{2,1,0:T(8,128)S(1)}, u32[]{:S(2)}, u32[]{:S(2)}) collective-permute-start(f32[4,64,128]{2,1,0:T(8,128)} %get-tuple-element.19), channel_id=1, source_target_pairs={{17,0},{18,1},{19,2},{20,3},{21,4},{22,5},{23,6},{24,7},{25,8},{26... | collective-permute-start | bytes 393224 | tf_op jit(solution)/shard_map/ppermute | solution.py:320
  28.4 5.3 %collective-permute-start.1 = (f32[17,64,128]{2,1,0:T(8,128)}, f32[17,64,128]{2,1,0:T(8,128)S(1)}, u32[]{:S(2)}, u32[]{:S(2)}) collective-permute-start(f32[17,64,128]{2,1,0:T(8,128)} %get-tuple-element.13), channel_id=1, source_target_pairs={{0,16},{16,32},{32,48},{48,64},{64,80},{80,96},{96,112},{112,128},... | collective-permute-start | bytes 1671176 | tf_op jit(solution)/shard_map/ppermute | solution.py:314
  33.8 0.1 reshape.196
  33.9 0.1 reshape.209
  33.9 0.1 add_reduce_fusion.1
  34.0 0.1 stack.15
  34.1 0.1 stack.16
  34.2 0.1 reduce.4
  34.4 0.1 select_reduce_fusion
  34.5 0.1 copy.72
  34.6 0.1 copy.74
  34.7 0.1 copy.73
  34.8 0.6 gather_fusion
  35.4 0.1 pad_add_fusion.4
  35.4 0.7 reshape.197.slot_ref
  36.1 0.0 collective-permute-done.cll_ref
  36.1 5.0 %collective-permute-start.3 = (f32[17,64,128]{2,1,0:T(8,128)}, f32[17,64,128]{2,1,0:T(8,128)S(1)}, u32[]{:S(2)}, u32[]{:S(2)}) collective-permute-start(f32[17,64,128]{2,1,0:T(8,128)} %get-tuple-element.15), channel_id=1, source_target_pairs={{0,1},{1,2},{2,3},{3,4},{4,5},{5,6},{6,7},{7,8},{8,9},{9,10},{10,1... | collective-permute-start | bytes 1671176 | tf_op jit(solution)/shard_map/ppermute | solution.py:316
  41.1 0.0 collective-permute-done.2.clh_ref
  41.1 1.9 %collective-permute-start.4 = (f32[17,64,128]{2,1,0:T(8,128)}, f32[17,64,128]{2,1,0:T(8,128)S(1)}, u32[]{:S(2)}, u32[]{:S(2)}) collective-permute-start(f32[17,64,128]{2,1,0:T(8,128)} %get-tuple-element.16), channel_id=1, source_target_pairs={{1,0},{2,1},{3,2},{4,3},{5,4},{6,5},{7,6},{8,7},{9,8},{10,9},{11,1... | collective-permute-start | bytes 1671176 | tf_op jit(solution)/shard_map/ppermute | solution.py:317
  43.1 0.0 collective-permute-done.5.chl_ref
  43.1 2.1 %collective-permute-start.6 = (f32[17,64,128]{2,1,0:T(8,128)}, f32[17,64,128]{2,1,0:T(8,128)S(1)}, u32[]{:S(2)}, u32[]{:S(2)}) collective-permute-start(f32[17,64,128]{2,1,0:T(8,128)} %get-tuple-element.18), channel_id=1, source_target_pairs={{16,0},{32,16},{48,32},{64,48},{80,64},{96,80},{112,96},{128,112},... | collective-permute-start | bytes 1671176 | tf_op jit(solution)/shard_map/ppermute | solution.py:315
  45.2 0.1 copy.80
  45.3 0.1 copy.81
  45.4 0.1 copy.82
  45.5 0.0 collective-permute-done.7.chh_ref
  45.5 0.1 copy.83
  45.6 0.0 collective-permute-done.1.xlo_ref
  45.6 0.1 convert_element_type.61
  45.7 0.1 copy.63
  45.8 2.1 %collective-permute-done.3.ylo_ref = f32[17,64,128]{2,1,0:T(8,128)S(1)} collective-permute-done((f32[17,64,128]{2,1,0:T(8,128)}, f32[17,64,128]{2,1,0:T(8,128)S(1)}, u32[]{:S(2)}, u32[]{:S(2)}) %collective-permute-start.3) | collective-permute-done | bytes 557088 | tf_op jit(solution)/shard_map/ppermute | solution.py:316
  47.9 0.1 convert_element_type.64
  48.0 0.1 copy.65
  48.1 5.6 %collective-permute-done.4.yhi_ref = f32[17,64,128]{2,1,0:T(8,128)S(1)} collective-permute-done((f32[17,64,128]{2,1,0:T(8,128)}, f32[17,64,128]{2,1,0:T(8,128)S(1)}, u32[]{:S(2)}, u32[]{:S(2)}) %collective-permute-start.4) | collective-permute-done | bytes 557088 | tf_op jit(solution)/shard_map/ppermute | solution.py:317
  53.7 0.1 convert_element_type.66
  53.8 0.1 copy.66
  53.9 5.6 %collective-permute-done.6.xhi_ref = f32[17,64,128]{2,1,0:T(8,128)S(1)} collective-permute-done((f32[17,64,128]{2,1,0:T(8,128)}, f32[17,64,128]{2,1,0:T(8,128)S(1)}, u32[]{:S(2)}, u32[]{:S(2)}) %collective-permute-start.6) | collective-permute-done | bytes 557088 | tf_op jit(solution)/shard_map/ppermute | solution.py:315
  59.6 0.1 convert_element_type.69
  59.6 0.1 copy.68
  59.7 0.1 fusion.1
  59.8 0.1 copy.70
  60.0 0.7 reshape.193.side_ref
  60.7 14.0 %shard_map.60 = (f32[32,1,128]{2,1,0:T(1,128)}, bf16[12,14,64,64]{3,2,1,0:T(8,128)(2,1)}) custom-call(s32[128]{0:T(128)} %reshape.193.side_ref, s32[48]{0:T(128)} %reshape.197.slot_ref, f32[4,4,64,64]{3,2,1,0:T(8,128)} %copy-done.2, f32[4,4,2,64,64]{4,3,2,1,0:T(8,128)} %convolution_bitcast_fusion.lead_ref, f32[4,4,64,64]{3,2,1,0:T(8,128)} %copy-done, ...), custom_call_target="tpu_custom_call" | custom-call | tf_op jit(solution)/shard_map/pallas_call | solution.py:271
  74.6 1.0 %slice_reduce_fusion = f32[32]{0:T(128)S(1)} fusion(f32[32,1,128]{2,1,0:T(1,128)} %get-tuple-element.20), kind=kLoop, calls=%fused_computation.5 | loop fusion | bytes 256 | tf_op jit(solution)/shard_map/slice | solution.py:286
  75.7 0.1 reshape_squeeze.3
  75.8 0.7 copy.75
  76.5 5.0 %reshape.198 = bf16[12,14,4096]{2,1,0:T(8,128)(2,1)} reshape(bf16[12,14,64,64]{3,2,1,0:T(8,128)(2,1)} %get-tuple-element.21) | data formatting | bytes 2752512 | tf_op jit(solution)/shard_map/reshape | solution.py:379
  (38 shorter events, 0.2 us)
Async XLA Ops:
  4.9 4.3 %copy-start = (f32[4,4,64,64]{3,2,1,0:T(8,128)}, f32[4,4,64,64]{3,2,1,0:T(8,128)S(1)}, u32[]{:S(2)}) copy-start(f32[4,4,64,64]{3,2,1,0:T(8,128)S(1)} %reshape.191.factor_ref) | copy-start | bytes 786436
  7.1 5.9 %copy-start.1 = (f32[4,4,2,64,64]{4,3,2,1,0:T(8,128)}, f32[4,4,2,64,64]{4,3,2,1,0:T(8,128)S(1)}, u32[]{:S(2)}) copy-start(f32[4,4,2,64,64]{4,3,2,1,0:T(8,128)S(1)} %reshape.192.minus_ref) | copy-start | bytes 1572868
  7.7 1.6 %copy-start.2 = (f32[4,4,64,64]{3,2,1,0:T(8,128)}, f32[4,4,64,64]{3,2,1,0:T(8,128)S(1)}, u32[]{:S(2)}) copy-start(f32[4,4,64,64]{3,2,1,0:T(8,128)S(1)} %convolution_multiply_fusion.fine_ref) | copy-start | bytes 786436
  7.7 26.1 %copy-start.12 = (s32[4,4]{1,0:T(4,128)S(1)}, s32[4,4]{1,0:T(4,128)}, u32[]{:S(2)}) copy-start(s32[4,4]{1,0:T(4,128)} %param.7) | copy-start | bytes 196
  7.7 26.2 %copy-start.11 = (s32[4,4,2]{1,2,0:T(2,128)S(1)}, s32[4,4,2]{1,2,0:T(2,128)}, u32[]{:S(2)}) copy-start(s32[4,4,2]{1,2,0:T(2,128)} %param.6) | copy-start | bytes 388
  12.9 23.2 %collective-permute-start = (f32[4,64,128]{2,1,0:T(8,128)}, f32[4,64,128]{2,1,0:T(8,128)S(1)}, u32[]{:S(2)}, u32[]{:S(2)}) collective-permute-start(f32[4,64,128]{2,1,0:T(8,128)} %get-tuple-element.12), channel_id=1, source_target_pairs={{0,17},{1,18},{2,19},{3,20},{4,21},{5,22},{6,23},{7,24},{8,25},{9,... | collective-permute-start | bytes 393224 | tf_op jit(solution)/shard_map/ppermute | solution.py:320
  18.8 22.3 %collective-permute-start.2 = (f32[4,64,128]{2,1,0:T(8,128)}, f32[4,64,128]{2,1,0:T(8,128)S(1)}, u32[]{:S(2)}, u32[]{:S(2)}) collective-permute-start(f32[4,64,128]{2,1,0:T(8,128)} %get-tuple-element.14), channel_id=1, source_target_pairs={{1,16},{2,17},{3,18},{4,19},{5,20},{6,21},{7,22},{8,23},{9,24},{10... | collective-permute-start | bytes 393224 | tf_op jit(solution)/shard_map/ppermute | solution.py:320
  20.8 22.3 %collective-permute-start.5 = (f32[4,64,128]{2,1,0:T(8,128)}, f32[4,64,128]{2,1,0:T(8,128)S(1)}, u32[]{:S(2)}, u32[]{:S(2)}) collective-permute-start(f32[4,64,128]{2,1,0:T(8,128)} %get-tuple-element.17), channel_id=1, source_target_pairs={{16,1},{17,2},{18,3},{19,4},{20,5},{21,6},{22,7},{23,8},{24,9},{25... | collective-permute-start | bytes 393224 | tf_op jit(solution)/shard_map/ppermute | solution.py:320
  26.5 19.0 %collective-permute-start.7 = (f32[4,64,128]{2,1,0:T(8,128)}, f32[4,64,128]{2,1,0:T(8,128)S(1)}, u32[]{:S(2)}, u32[]{:S(2)}) collective-permute-start(f32[4,64,128]{2,1,0:T(8,128)} %get-tuple-element.19), channel_id=1, source_target_pairs={{17,0},{18,1},{19,2},{20,3},{21,4},{22,5},{23,6},{24,7},{25,8},{26... | collective-permute-start | bytes 393224 | tf_op jit(solution)/shard_map/ppermute | solution.py:320
  28.4 17.2 %collective-permute-start.1 = (f32[17,64,128]{2,1,0:T(8,128)}, f32[17,64,128]{2,1,0:T(8,128)S(1)}, u32[]{:S(2)}, u32[]{:S(2)}) collective-permute-start(f32[17,64,128]{2,1,0:T(8,128)} %get-tuple-element.13), channel_id=1, source_target_pairs={{0,16},{16,32},{32,48},{48,64},{64,80},{80,96},{96,112},{112,128},... | collective-permute-start | bytes 1671176 | tf_op jit(solution)/shard_map/ppermute | solution.py:314
  36.1 24.5 %copy-start.7 = (f32[4,64,128]{2,1,0:T(8,128)}, f32[4,64,128]{2,1,0:T(8,128)S(1)}, u32[]{:S(2)}) copy-start(f32[4,64,128]{2,1,0:T(8,128)S(1)} %collective-permute-done.cll_ref) | copy-start | bytes 393220
  36.1 11.8 %collective-permute-start.3 = (f32[17,64,128]{2,1,0:T(8,128)}, f32[17,64,128]{2,1,0:T(8,128)S(1)}, u32[]{:S(2)}, u32[]{:S(2)}) collective-permute-start(f32[17,64,128]{2,1,0:T(8,128)} %get-tuple-element.15), channel_id=1, source_target_pairs={{0,1},{1,2},{2,3},{3,4},{4,5},{5,6},{6,7},{7,8},{8,9},{9,10},{10,1... | collective-permute-start | bytes 1671176 | tf_op jit(solution)/shard_map/ppermute | solution.py:316
  41.1 19.5 %copy-start.8 = (f32[4,64,128]{2,1,0:T(8,128)}, f32[4,64,128]{2,1,0:T(8,128)S(1)}, u32[]{:S(2)}) copy-start(f32[4,64,128]{2,1,0:T(8,128)S(1)} %collective-permute-done.2.clh_ref) | copy-start | bytes 393220
  41.1 12.6 %collective-permute-start.4 = (f32[17,64,128]{2,1,0:T(8,128)}, f32[17,64,128]{2,1,0:T(8,128)S(1)}, u32[]{:S(2)}, u32[]{:S(2)}) collective-permute-start(f32[17,64,128]{2,1,0:T(8,128)} %get-tuple-element.16), channel_id=1, source_target_pairs={{1,0},{2,1},{3,2},{4,3},{5,4},{6,5},{7,6},{8,7},{9,8},{10,9},{11,1... | collective-permute-start | bytes 1671176 | tf_op jit(solution)/shard_map/ppermute | solution.py:317
  43.1 17.5 %copy-start.9 = (f32[4,64,128]{2,1,0:T(8,128)}, f32[4,64,128]{2,1,0:T(8,128)S(1)}, u32[]{:S(2)}) copy-start(f32[4,64,128]{2,1,0:T(8,128)S(1)} %collective-permute-done.5.chl_ref) | copy-start | bytes 393220
  43.1 16.4 %collective-permute-start.6 = (f32[17,64,128]{2,1,0:T(8,128)}, f32[17,64,128]{2,1,0:T(8,128)S(1)}, u32[]{:S(2)}, u32[]{:S(2)}) collective-permute-start(f32[17,64,128]{2,1,0:T(8,128)} %get-tuple-element.18), channel_id=1, source_target_pairs={{16,0},{32,16},{48,32},{64,48},{80,64},{96,80},{112,96},{128,112},... | collective-permute-start | bytes 1671176 | tf_op jit(solution)/shard_map/ppermute | solution.py:315
  45.5 15.1 %copy-start.10 = (f32[4,64,128]{2,1,0:T(8,128)}, f32[4,64,128]{2,1,0:T(8,128)S(1)}, u32[]{:S(2)}) copy-start(f32[4,64,128]{2,1,0:T(8,128)S(1)} %collective-permute-done.7.chh_ref) | copy-start | bytes 393220
  45.6 15.0 %copy-start.3 = (f32[17,64,128]{2,1,0:T(8,128)}, f32[17,64,128]{2,1,0:T(8,128)S(1)}, u32[]{:S(2)}) copy-start(f32[17,64,128]{2,1,0:T(8,128)S(1)} %collective-permute-done.1.xlo_ref) | copy-start | bytes 1671172
  47.9 12.8 %copy-start.4 = (f32[17,64,128]{2,1,0:T(8,128)}, f32[17,64,128]{2,1,0:T(8,128)S(1)}, u32[]{:S(2)}) copy-start(f32[17,64,128]{2,1,0:T(8,128)S(1)} %collective-permute-done.3.ylo_ref) | copy-start | bytes 1671172
  53.7 6.9 %copy-start.5 = (f32[17,64,128]{2,1,0:T(8,128)}, f32[17,64,128]{2,1,0:T(8,128)S(1)}, u32[]{:S(2)}) copy-start(f32[17,64,128]{2,1,0:T(8,128)S(1)} %collective-permute-done.4.yhi_ref) | copy-start | bytes 1671172
  59.5 1.1 %copy-start.6 = (f32[17,64,128]{2,1,0:T(8,128)}, f32[17,64,128]{2,1,0:T(8,128)S(1)}, u32[]{:S(2)}) copy-start(f32[17,64,128]{2,1,0:T(8,128)S(1)} %collective-permute-done.6.xhi_ref) | copy-start | bytes 1671172
where the time goes:
time: 82.1 us; the launch traced here: 81.5 us
  starting transfers between devices  29.8 us (36%)
  Pallas kernels  17.6 us (21%)
  local copies, waits for them, and re-layouts  14 us (17%)
  waiting for transfers between devices  13.3 us (16%)
  other arithmetic  3.72 us (5%)
  matrix products  2.13 us (3%)
  between operations  0.9 us (1%)
    ppermute x4, starting transfers between devices, on_device(): lax.ppermute(buffer, ('gx', 'gy'), corner_pairs(n_gx, n_gy, *step))  15.5 us
    pallas_call x1, Pallas kernels, local_compute(): pl.pallas_call(local_kernel, out_shape=(jax.ShapeDtypeStruct((nx * ny * 2...  14 us
    ppermute x1, waiting for transfers between devices, on_device(): from_yhi = lax.ppermute(packed[3], 'gy', shift_pairs(n_gy, -1))  5.6 us
    ppermute x1, waiting for transfers between devices, on_device(): from_xhi = lax.ppermute(packed[1], 'gx', shift_pairs(n_gx, -1))  5.59 us
    ppermute x1, starting transfers between devices, on_device(): from_xlo = lax.ppermute(packed[0], 'gx', shift_pairs(n_gx, 1))  5.31 us
    reshape x1, local copies, waits for them, and re-layouts, on_device(): return (strong, restrict.reshape(CAP, 14, flat))  5.02 us
    ppermute x1, starting transfers between devices, on_device(): from_ylo = lax.ppermute(packed[2], 'gy', shift_pairs(n_gy, 1))  5.01 us
    pallas_call x1, Pallas kernels, pack_buffers(): pl.pallas_call(pack_kernel, out_shape=tuple(shapes), in_specs=[smem, vmem...  3.67 us
  transfers between devices with their start and end apart: 8, of which 3 were waited for; matrix products, arithmetic and copies ran while one was open for 4% of the time, Pallas kernels for 0%

commit v1 on v0

--- a/solution.py
+++ b/solution.py
@@ -9,10 +9,6 @@
 
 CAP = 12
 PREC = lax.Precision.HIGH
-
-
-def matmul(left_block, right_block):
-    return jnp.einsum("...ij,...jk->...ik", left_block, right_block, precision=PREC)
 
 
 def left_gram(left_block, right_block):
@@ -157,7 +153,8 @@
             up = gg[i + 2 * s, j + 1] if d == 0 else gg[i + 1, j + 2 * s]
             scaled = dot3(split(dot3(factor, split(minus_ref[i, j, d]))), split(up), True)
             total = jnp.sum(scaled * scaled, axis=(0, 1), keepdims=True)
-            strong_ref[p * 2 + d] = jnp.broadcast_to(total * (1.0 / scaled.size), (1, 128))
+            strong_ref[pl.ds(p * 2 + d, 1), :] = jnp.broadcast_to(total * (1.0 / scaled.size),
+                                                                 (1, 128))
         return carry
 
     lax.fori_loop(0, nx * ny, strong_step, 0, unroll=True)
@@ -221,9 +218,14 @@
     return tile
 
 
-def pack_kernel(side_ref, fine_ref, lead_ref, factor_ref, *out_refs):
+def pack_kernel(side_ref, fine_ref, minus_ref, factor_ref, lead_ref, *out_refs):
     nx, ny = fine_ref.shape[0], fine_ref.shape[1]
     width = fine_ref.shape[-1]
+    for i in range(nx):
+        for j in range(ny):
+            fine = split(fine_ref[i, j])
+            for e in range(2):
+                lead_ref[i, j, e] = dot3(fine, split(minus_ref[i, j, e]))
     named = {"fine": fine_ref, "lead": lead_ref, "factor": factor_ref}
     for out, side in zip(out_refs[:4], ("xhi", "xlo", "yhi", "ylo")):
         sources, codes = face_sources(nx, ny, side)
@@ -244,7 +246,7 @@
                                           out.shape[1:])
 
 
-def pack_buffers(stencil, fine_own, lead_own, factor_own):
+def pack_buffers(stencil, fine_own, minus_own, factor_own):
     nx, ny = fine_own.shape[:2]
     blk = fine_own.shape[2:]
     face_count = len(face_sources(nx, ny, "xhi")[0]) + 1
@@ -254,12 +256,13 @@
     paired = lambda count: jax.ShapeDtypeStruct(((count + 1) // 2, blk[0], 2 * blk[1]), jnp.float32)
     shapes = [paired(face_count)] * 2 + [paired(face_y_count)] * 2
     shapes += [paired(7)] * 4
+    shapes = [jax.ShapeDtypeStruct(minus_own.shape, jnp.float32)] + shapes
     return pl.pallas_call(
         pack_kernel,
         out_shape=tuple(shapes),
         in_specs=[smem, vmem, vmem, vmem],
-        out_specs=tuple([vmem] * 8),
-    )(stencil.reshape(-1), fine_own, lead_own, factor_own)
+        out_specs=tuple([vmem] * 9),
+    )(stencil.reshape(-1), fine_own, minus_own, factor_own)
 
 
 def local_compute(side_flat, slot_table, fine_own, lead_own, factor_own, minus_own, buffers):
@@ -270,7 +273,7 @@
     f32 = jnp.float32
     strong, restrict = pl.pallas_call(
         local_kernel,
-        out_shape=(jax.ShapeDtypeStruct((nx * ny * 2, 1, 128), f32),
+        out_shape=(jax.ShapeDtypeStruct((nx * ny * 2, 128), f32),
                    jax.ShapeDtypeStruct((CAP, 14) + blk, jnp.bfloat16)),
         in_specs=[smem, smem] + [vmem] * (4 + len(buffers)),
         out_specs=(vmem, vmem),
@@ -283,7 +286,7 @@
         ],
         compiler_params=pltpu.CompilerParams(vmem_limit_bytes=60 * 1024 * 1024),
     )(side_flat, slot_table, fine_own, lead_own, factor_own, minus_own, *buffers)
-    return strong[:, 0, 0].reshape(nx, ny, 2), restrict
+    return strong[:, 0].reshape(nx, ny, 2), restrict
 
 
 def on_device(inv_factors, couplings, stencil, coarse):
@@ -308,9 +311,8 @@
     fine_own = (1 - coarse).astype(jnp.float32)[:, :, None, None] * left_gram(
         factor_own, factor_own
     )
-    lead_own = matmul(fine_own[:, :, None], minus_own)
-
-    packed = pack_buffers(stencil, fine_own, lead_own, factor_own)
+
+    lead_own, *packed = pack_buffers(stencil, fine_own, minus_own, factor_own)
     from_xlo = lax.ppermute(packed[0], "gx", shift_pairs(n_gx, 1))
     from_xhi = lax.ppermute(packed[1], "gx", shift_pairs(n_gx, -1))
     from_ylo = lax.ppermute(packed[2], "gy", shift_pairs(n_gy, 1))

time: 82.1 us -> 82.6 us (level)
    dot_general x1 -> x0, matrix products: 1.54 us -> none  [matmul(): jnp.einsum('...ij,...jk->...ik', left_block, right_block, precision=PREC)]
    reshape x1, local copies, waits for them, and re-layouts: 0.62 us -> 1.6 us  [on_device(): (couplings * (-reach.astype(jnp.float32))[:, :, :, None]).reshape((nx, ny...]
    unnamed x32 -> x28, local copies, waits for them, and re-layouts: 1.93 us -> 1.92 us
where the time goes in v1:
time: 82.6 us; the launch traced here: 82 us
  starting transfers between devices  29.8 us (36%)
  Pallas kernels  18.1 us (22%)
  local copies, waits for them, and re-layouts  14.8 us (18%)
  waiting for transfers between devices  13.3 us (16%)
  other arithmetic  3.72 us (5%)
  matrix products  1.4 us (2%)
  between operations  0.89 us (1%)
    ppermute x4, starting transfers between devices, on_device(): lax.ppermute(buffer, ('gx', 'gy'), corner_pairs(n_gx, n_gy, *step))  15.5 us
    pallas_call x1, Pallas kernels, local_compute(): pl.pallas_call(local_kernel, out_shape=(jax.ShapeDtypeStruct((nx * ny * 2...  14 us
    ppermute x1, waiting for transfers between devices, on_device(): from_yhi = lax.ppermute(packed[3], 'gy', shift_pairs(n_gy, -1))  5.6 us
    ppermute x1, waiting for transfers between devices, on_device(): from_xhi = lax.ppermute(packed[1], 'gx', shift_pairs(n_gx, -1))  5.59 us
    ppermute x1, starting transfers between devices, on_device(): from_xlo = lax.ppermute(packed[0], 'gx', shift_pairs(n_gx, 1))  5.31 us
    reshape x1, local copies, waits for them, and re-layouts, on_device(): return (strong, restrict.reshape(CAP, 14, flat))  5.02 us
    ppermute x1, starting transfers between devices, on_device(): from_ylo = lax.ppermute(packed[2], 'gy', shift_pairs(n_gy, 1))  5.01 us
    pallas_call x1, Pallas kernels, pack_buffers(): pl.pallas_call(pack_kernel, out_shape=tuple(shapes), in_specs=[smem, vmem...  4.13 us
  transfers between devices with their start and end apart: 8, of which 3 were waited for; matrix products, arithmetic and copies ran while one was open for 4% of the time, Pallas kernels for 0%

profile of v1, /device:TPU:121, one launch (start us, length us, event | category | flops | bytes accessed | tf_op | source)
XLA Modules:
  0.0 82.0 jit_solution(11083472377574213382)
XLA Ops:
  0.6 0.7 subtract_convert_fusion
  1.3 0.8 copy.51
  2.1 0.8 %compare_and_fusion.1 = (pred[4,4,1]{1,2,0:T(4,128)(4,1)S(1)}, pred[4,4,1]{1,2,0:T(4,128)(4,1)S(1)}) fusion(s32[4]{0:T(128)S(1)} %get-tuple-element.39, s32[4,4,2]{1,2,0:T(2,128)} %param.6, s32[4]{0:T(128)S(1)} %get-tuple-element.38), kind=kLoop, calls=%fused_computation.17 | loop fusion | flops 192 | bytes 192 | tf_op jit(solution)/shard_map/and | solution.py:305
  3.0 0.1 copy.53
  3.1 0.6 reshape.190.side_ref
  3.7 1.2 %reshape.191.factor_ref = f32[4,4,64,64]{3,2,1,0:T(8,128)S(1)} reshape(f32[4,4,4096]{2,1,0:T(4,128)} %param.4) | data formatting | bytes 524288 | tf_op jit(solution)/shard_map/reshape | solution.py:310
  4.9 1.5 %broadcast_multiply_fusion = f32[4,4,2,4096]{3,2,1,0:T(2,128)S(1)} fusion(f32[4,4,2,4096]{3,2,1,0:T(2,128)} %param.5, f32[4,4,2]{2,1,0:T(4,128)S(1)} %copy.53), kind=kLoop, calls=%fused_computation.2 | loop fusion | flops 131072 | bytes 1048704 | tf_op jit(solution)/shard_map/mul | solution.py:307
  6.5 0.0 copy-start.10
  6.5 0.0 copy-start.9
  6.5 1.6 %reshape.192.minus_ref = f32[4,4,2,64,64]{4,3,2,1,0:T(8,128)} reshape(f32[4,4,2,4096]{3,2,1,0:T(2,128)S(1)} %broadcast_multiply_fusion) | data formatting | bytes 1048576 | tf_op jit(solution)/shard_map/reshape | solution.py:307
  8.1 1.4 %convolution_multiply_fusion.fine_ref = f32[4,4,64,64]{3,2,1,0:T(8,128)} fusion(f32[4,4,64,64]{3,2,1,0:T(8,128)S(1)} %reshape.191.factor_ref, f32[4,4]{1,0:T(4,128)S(1)} %subtract_convert_fusion), kind=kOutput, calls=%fused_computation.1 | convolution fusion | flops 25231360 | bytes 524352 | tf_op jit(solution)/shard_map/...ji,...jk->...ik/dot_general | solution.py:15
  9.5 4.1 %shard_map.59 = (f32[4,4,2,64,64]{4,3,2,1,0:T(8,128)}, f32[17,64,128]{2,1,0:T(8,128)}, f32[17,64,128]{2,1,0:T(8,128)}, f32[17,64,128]{2,1,0:T(8,128)}, f32[17,64...) custom-call(s32[32]{0:T(128)} %reshape.190.side_ref, ...), custom_call_target="tpu_custom_call" | custom-call | tf_op jit(solution)/shard_map/pallas_call | solution.py:260
  13.6 5.9 %collective-permute-start = (f32[4,64,128]{2,1,0:T(8,128)}, f32[4,64,128]{2,1,0:T(8,128)S(1)}, u32[]{:S(2)}, u32[]{:S(2)}) collective-permute-start(f32[4,64,128]{2,1,0:T(8,128)} %get-tuple-element.13), channel_id=1, source_target_pairs={{0,17},{1,18},{2,19},{3,20},{4,21},{5,22},{6,23},{7,24},{8,25},{9,... | collective-permute-start | bytes 393224 | tf_op jit(solution)/shard_map/ppermute | solution.py:322
  19.5 1.9 %collective-permute-start.2 = (f32[4,64,128]{2,1,0:T(8,128)}, f32[4,64,128]{2,1,0:T(8,128)S(1)}, u32[]{:S(2)}, u32[]{:S(2)}) collective-permute-start(f32[4,64,128]{2,1,0:T(8,128)} %get-tuple-element.15), channel_id=1, source_target_pairs={{1,16},{2,17},{3,18},{4,19},{5,20},{6,21},{7,22},{8,23},{9,24},{10... | collective-permute-start | bytes 393224 | tf_op jit(solution)/shard_map/ppermute | solution.py:322
  21.4 5.8 %collective-permute-start.5 = (f32[4,64,128]{2,1,0:T(8,128)}, f32[4,64,128]{2,1,0:T(8,128)S(1)}, u32[]{:S(2)}, u32[]{:S(2)}) collective-permute-start(f32[4,64,128]{2,1,0:T(8,128)} %get-tuple-element.18), channel_id=1, source_target_pairs={{16,1},{17,2},{18,3},{19,4},{20,5},{21,6},{22,7},{23,8},{24,9},{25... | collective-permute-start | bytes 393224 | tf_op jit(solution)/shard_map/ppermute | solution.py:322
  27.2 1.9 %collective-permute-start.7 = (f32[4,64,128]{2,1,0:T(8,128)}, f32[4,64,128]{2,1,0:T(8,128)S(1)}, u32[]{:S(2)}, u32[]{:S(2)}) collective-permute-start(f32[4,64,128]{2,1,0:T(8,128)} %get-tuple-element.20), channel_id=1, source_target_pairs={{17,0},{18,1},{19,2},{20,3},{21,4},{22,5},{23,6},{24,7},{25,8},{26... | collective-permute-start | bytes 393224 | tf_op jit(solution)/shard_map/ppermute | solution.py:322
  29.1 5.3 %collective-permute-start.1 = (f32[17,64,128]{2,1,0:T(8,128)}, f32[17,64,128]{2,1,0:T(8,128)S(1)}, u32[]{:S(2)}, u32[]{:S(2)}) collective-permute-start(f32[17,64,128]{2,1,0:T(8,128)} %get-tuple-element.14), channel_id=1, source_target_pairs={{0,16},{16,32},{32,48},{48,64},{64,80},{80,96},{96,112},{112,128},... | collective-permute-start | bytes 1671176 | tf_op jit(solution)/shard_map/ppermute | solution.py:316
  34.4 0.0 copy-done.10
  34.5 0.1 reshape.196
  34.5 0.1 reshape.208
  34.6 0.0 copy-done.9
  34.6 0.1 add_reduce_fusion.1
  34.7 0.1 stack.15
  34.8 0.1 stack.16
  34.9 0.1 reduce.4
  35.1 0.1 select_reduce_fusion
  35.2 0.1 copy.64
  35.3 0.1 copy.66
  35.4 0.1 copy.65
  35.5 0.6 gather_fusion
  36.0 0.1 pad_add_fusion.4
  36.1 0.7 reshape.197.slot_ref
  36.8 0.0 collective-permute-done.cll_ref
  36.8 5.0 %collective-permute-start.3 = (f32[17,64,128]{2,1,0:T(8,128)}, f32[17,64,128]{2,1,0:T(8,128)S(1)}, u32[]{:S(2)}, u32[]{:S(2)}) collective-permute-start(f32[17,64,128]{2,1,0:T(8,128)} %get-tuple-element.16), channel_id=1, source_target_pairs={{0,1},{1,2},{2,3},{3,4},{4,5},{5,6},{6,7},{7,8},{8,9},{9,10},{10,1... | collective-permute-start | bytes 1671176 | tf_op jit(solution)/shard_map/ppermute | solution.py:318
  41.8 0.0 collective-permute-done.2.clh_ref
  41.8 1.9 %collective-permute-start.4 = (f32[17,64,128]{2,1,0:T(8,128)}, f32[17,64,128]{2,1,0:T(8,128)S(1)}, u32[]{:S(2)}, u32[]{:S(2)}) collective-permute-start(f32[17,64,128]{2,1,0:T(8,128)} %get-tuple-element.17), channel_id=1, source_target_pairs={{1,0},{2,1},{3,2},{4,3},{5,4},{6,5},{7,6},{8,7},{9,8},{10,9},{11,1... | collective-permute-start | bytes 1671176 | tf_op jit(solution)/shard_map/ppermute | solution.py:319
  43.8 0.0 collective-permute-done.5.chl_ref
  43.8 2.1 %collective-permute-start.6 = (f32[17,64,128]{2,1,0:T(8,128)}, f32[17,64,128]{2,1,0:T(8,128)S(1)}, u32[]{:S(2)}, u32[]{:S(2)}) collective-permute-start(f32[17,64,128]{2,1,0:T(8,128)} %get-tuple-element.19), channel_id=1, source_target_pairs={{16,0},{32,16},{48,32},{64,48},{80,64},{96,80},{112,96},{128,112},... | collective-permute-start | bytes 1671176 | tf_op jit(solution)/shard_map/ppermute | solution.py:317
  45.9 0.1 copy.69
  46.0 0.1 copy.70
  46.1 0.1 copy.71
  46.2 0.0 collective-permute-done.7.chh_ref
  46.2 0.1 copy.72
  46.3 0.0 collective-permute-done.1.xlo_ref
  46.3 0.1 convert_element_type.61
  46.4 0.1 copy.55
  46.5 2.1 %collective-permute-done.3.ylo_ref = f32[17,64,128]{2,1,0:T(8,128)S(1)} collective-permute-done((f32[17,64,128]{2,1,0:T(8,128)}, f32[17,64,128]{2,1,0:T(8,128)S(1)}, u32[]{:S(2)}, u32[]{:S(2)}) %collective-permute-start.3) | collective-permute-done | bytes 557088 | tf_op jit(solution)/shard_map/ppermute | solution.py:318
  48.6 0.1 convert_element_type.64
  48.7 0.1 copy.57
  48.8 5.6 %collective-permute-done.4.yhi_ref = f32[17,64,128]{2,1,0:T(8,128)S(1)} collective-permute-done((f32[17,64,128]{2,1,0:T(8,128)}, f32[17,64,128]{2,1,0:T(8,128)S(1)}, u32[]{:S(2)}, u32[]{:S(2)}) %collective-permute-start.4) | collective-permute-done | bytes 557088 | tf_op jit(solution)/shard_map/ppermute | solution.py:319
  54.4 0.1 convert_element_type.66
  54.5 0.1 copy.58
  54.6 5.6 %collective-permute-done.6.xhi_ref = f32[17,64,128]{2,1,0:T(8,128)S(1)} collective-permute-done((f32[17,64,128]{2,1,0:T(8,128)}, f32[17,64,128]{2,1,0:T(8,128)S(1)}, u32[]{:S(2)}, u32[]{:S(2)}) %collective-permute-start.6) | collective-permute-done | bytes 557088 | tf_op jit(solution)/shard_map/ppermute | solution.py:317
  60.2 0.1 convert_element_type.69
  60.3 0.1 copy.60
  60.4 0.1 fusion
  60.5 0.1 copy.62
  60.6 0.7 reshape.193.side_ref
  61.3 0.0 copy-done.5
  61.3 14.0 %shard_map.60 = (f32[32,128]{1,0:T(8,128)}, bf16[12,14,64,64]{3,2,1,0:T(8,128)(2,1)}) custom-call(s32[128]{0:T(128)} %reshape.193.side_ref, s32[48]{0:T(128)} %reshape.197.slot_ref, f32[4,4,64,64]{3,2,1,0:T(8,128)} %convolution_multiply_fusion.fine_ref, f32[4,4,2,64,64]{4,3,2,1,0:T(8,128)} %get-tuple-element.21.lead_ref, f32[4,4,64,64]{3,2,1,0:T(8,128)} %copy-done, ...), custom_call_target="tpu_custom_call" | custom-call | tf_op jit(solution)/shard_map/pallas_call | solution.py:274
  75.3 0.8 %slice_reduce_fusion = f32[32]{0:T(128)S(1)} fusion(f32[32,128]{1,0:T(8,128)} %get-tuple-element.22), kind=kLoop, calls=%fused_computation.3 | loop fusion | bytes 256 | tf_op jit(solution)/shard_map/slice | solution.py:289
  76.1 0.1 reshape_squeeze.3
  76.2 0.7 copy.67
  77.0 5.0 %reshape.198 = bf16[12,14,4096]{2,1,0:T(8,128)(2,1)} reshape(bf16[12,14,64,64]{3,2,1,0:T(8,128)(2,1)} %get-tuple-element.23) | data formatting | bytes 2752512 | tf_op jit(solution)/shard_map/reshape | solution.py:381
  (33 shorter events, 0.2 us)
Async XLA Ops:
  4.9 4.5 %copy-start = (f32[4,4,64,64]{3,2,1,0:T(8,128)}, f32[4,4,64,64]{3,2,1,0:T(8,128)S(1)}, u32[]{:S(2)}) copy-start(f32[4,4,64,64]{3,2,1,0:T(8,128)S(1)} %reshape.191.factor_ref) | copy-start | bytes 786436
  6.5 28.0 %copy-start.10 = (s32[4,4]{1,0:T(4,128)S(1)}, s32[4,4]{1,0:T(4,128)}, u32[]{:S(2)}) copy-start(s32[4,4]{1,0:T(4,128)} %param.7) | copy-start | bytes 196
  6.5 28.2 %copy-start.9 = (s32[4,4,2]{1,2,0:T(2,128)S(1)}, s32[4,4,2]{1,2,0:T(2,128)}, u32[]{:S(2)}) copy-start(s32[4,4,2]{1,2,0:T(2,128)} %param.6) | copy-start | bytes 388
  13.6 23.2 %collective-permute-start = (f32[4,64,128]{2,1,0:T(8,128)}, f32[4,64,128]{2,1,0:T(8,128)S(1)}, u32[]{:S(2)}, u32[]{:S(2)}) collective-permute-start(f32[4,64,128]{2,1,0:T(8,128)} %get-tuple-element.13), channel_id=1, source_target_pairs={{0,17},{1,18},{2,19},{3,20},{4,21},{5,22},{6,23},{7,24},{8,25},{9,... | collective-permute-start | bytes 393224 | tf_op jit(solution)/shard_map/ppermute | solution.py:322
  19.5 22.3 %collective-permute-start.2 = (f32[4,64,128]{2,1,0:T(8,128)}, f32[4,64,128]{2,1,0:T(8,128)S(1)}, u32[]{:S(2)}, u32[]{:S(2)}) collective-permute-start(f32[4,64,128]{2,1,0:T(8,128)} %get-tuple-element.15), channel_id=1, source_target_pairs={{1,16},{2,17},{3,18},{4,19},{5,20},{6,21},{7,22},{8,23},{9,24},{10... | collective-permute-start | bytes 393224 | tf_op jit(solution)/shard_map/ppermute | solution.py:322
  21.4 22.3 %collective-permute-start.5 = (f32[4,64,128]{2,1,0:T(8,128)}, f32[4,64,128]{2,1,0:T(8,128)S(1)}, u32[]{:S(2)}, u32[]{:S(2)}) collective-permute-start(f32[4,64,128]{2,1,0:T(8,128)} %get-tuple-element.18), channel_id=1, source_target_pairs={{16,1},{17,2},{18,3},{19,4},{20,5},{21,6},{22,7},{23,8},{24,9},{25... | collective-permute-start | bytes 393224 | tf_op jit(solution)/shard_map/ppermute | solution.py:322
  27.2 19.0 %collective-permute-start.7 = (f32[4,64,128]{2,1,0:T(8,128)}, f32[4,64,128]{2,1,0:T(8,128)S(1)}, u32[]{:S(2)}, u32[]{:S(2)}) collective-permute-start(f32[4,64,128]{2,1,0:T(8,128)} %get-tuple-element.20), channel_id=1, source_target_pairs={{17,0},{18,1},{19,2},{20,3},{21,4},{22,5},{23,6},{24,7},{25,8},{26... | collective-permute-start | bytes 393224 | tf_op jit(solution)/shard_map/ppermute | solution.py:322
  29.1 17.2 %collective-permute-start.1 = (f32[17,64,128]{2,1,0:T(8,128)}, f32[17,64,128]{2,1,0:T(8,128)S(1)}, u32[]{:S(2)}, u32[]{:S(2)}) collective-permute-start(f32[17,64,128]{2,1,0:T(8,128)} %get-tuple-element.14), channel_id=1, source_target_pairs={{0,16},{16,32},{32,48},{48,64},{64,80},{80,96},{96,112},{112,128},... | collective-permute-start | bytes 1671176 | tf_op jit(solution)/shard_map/ppermute | solution.py:316
  36.8 24.5 %copy-start.5 = (f32[4,64,128]{2,1,0:T(8,128)}, f32[4,64,128]{2,1,0:T(8,128)S(1)}, u32[]{:S(2)}) copy-start(f32[4,64,128]{2,1,0:T(8,128)S(1)} %collective-permute-done.cll_ref) | copy-start | bytes 393220
  36.8 11.8 %collective-permute-start.3 = (f32[17,64,128]{2,1,0:T(8,128)}, f32[17,64,128]{2,1,0:T(8,128)S(1)}, u32[]{:S(2)}, u32[]{:S(2)}) collective-permute-start(f32[17,64,128]{2,1,0:T(8,128)} %get-tuple-element.16), channel_id=1, source_target_pairs={{0,1},{1,2},{2,3},{3,4},{4,5},{5,6},{6,7},{7,8},{8,9},{9,10},{10,1... | collective-permute-start | bytes 1671176 | tf_op jit(solution)/shard_map/ppermute | solution.py:318
  41.8 19.5 %copy-start.6 = (f32[4,64,128]{2,1,0:T(8,128)}, f32[4,64,128]{2,1,0:T(8,128)S(1)}, u32[]{:S(2)}) copy-start(f32[4,64,128]{2,1,0:T(8,128)S(1)} %collective-permute-done.2.clh_ref) | copy-start | bytes 393220
  41.8 12.6 %collective-permute-start.4 = (f32[17,64,128]{2,1,0:T(8,128)}, f32[17,64,128]{2,1,0:T(8,128)S(1)}, u32[]{:S(2)}, u32[]{:S(2)}) collective-permute-start(f32[17,64,128]{2,1,0:T(8,128)} %get-tuple-element.17), channel_id=1, source_target_pairs={{1,0},{2,1},{3,2},{4,3},{5,4},{6,5},{7,6},{8,7},{9,8},{10,9},{11,1... | collective-permute-start | bytes 1671176 | tf_op jit(solution)/shard_map/ppermute | solution.py:319
  43.8 17.5 %copy-start.7 = (f32[4,64,128]{2,1,0:T(8,128)}, f32[4,64,128]{2,1,0:T(8,128)S(1)}, u32[]{:S(2)}) copy-start(f32[4,64,128]{2,1,0:T(8,128)S(1)} %collective-permute-done.5.chl_ref) | copy-start | bytes 393220
  43.8 16.4 %collective-permute-start.6 = (f32[17,64,128]{2,1,0:T(8,128)}, f32[17,64,128]{2,1,0:T(8,128)S(1)}, u32[]{:S(2)}, u32[]{:S(2)}) collective-permute-start(f32[17,64,128]{2,1,0:T(8,128)} %get-tuple-element.19), channel_id=1, source_target_pairs={{16,0},{32,16},{48,32},{64,48},{80,64},{96,80},{112,96},{128,112},... | collective-permute-start | bytes 1671176 | tf_op jit(solution)/shard_map/ppermute | solution.py:317
  46.2 15.1 %copy-start.8 = (f32[4,64,128]{2,1,0:T(8,128)}, f32[4,64,128]{2,1,0:T(8,128)S(1)}, u32[]{:S(2)}) copy-start(f32[4,64,128]{2,1,0:T(8,128)S(1)} %collective-permute-done.7.chh_ref) | copy-start | bytes 393220
  46.3 15.0 %copy-start.1 = (f32[17,64,128]{2,1,0:T(8,128)}, f32[17,64,128]{2,1,0:T(8,128)S(1)}, u32[]{:S(2)}) copy-start(f32[17,64,128]{2,1,0:T(8,128)S(1)} %collective-permute-done.1.xlo_ref) | copy-start | bytes 1671172
  48.6 12.8 %copy-start.2 = (f32[17,64,128]{2,1,0:T(8,128)}, f32[17,64,128]{2,1,0:T(8,128)S(1)}, u32[]{:S(2)}) copy-start(f32[17,64,128]{2,1,0:T(8,128)S(1)} %collective-permute-done.3.ylo_ref) | copy-start | bytes 1671172
  54.4 6.9 %copy-start.3 = (f32[17,64,128]{2,1,0:T(8,128)}, f32[17,64,128]{2,1,0:T(8,128)S(1)}, u32[]{:S(2)}) copy-start(f32[17,64,128]{2,1,0:T(8,128)S(1)} %collective-permute-done.4.yhi_ref) | copy-start | bytes 1671172
  60.2 1.1 %copy-start.4 = (f32[17,64,128]{2,1,0:T(8,128)}, f32[17,64,128]{2,1,0:T(8,128)S(1)}, u32[]{:S(2)}) copy-start(f32[17,64,128]{2,1,0:T(8,128)S(1)} %collective-permute-done.6.xhi_ref) | copy-start | bytes 1671172

commit v2 on v1

--- a/solution.py
+++ b/solution.py
@@ -144,7 +144,7 @@
                 zg[i, j, 2 + 3 * e] = dot3(lead, split(yg[ui, uj, 0]))
                 zg[i, j, 3 + 3 * e] = dot3(lead, split(yg[ui, uj, 1]))
 
-    def strong_step(p, carry):
+    for p in range(nx * ny):
         i = p // ny
         j = p % ny
         factor = split(factor_ref[i, j])
@@ -155,9 +155,7 @@
             total = jnp.sum(scaled * scaled, axis=(0, 1), keepdims=True)
             strong_ref[pl.ds(p * 2 + d, 1), :] = jnp.broadcast_to(total * (1.0 / scaled.size),
                                                                  (1, 128))
-        return carry
-
-    lax.fori_loop(0, nx * ny, strong_step, 0, unroll=True)
+
 
     def slot_step(s, carry):
         cell = slot_ref[s * 4]
@@ -304,9 +302,9 @@
     reach = jnp.stack(
         [(target_x >= 0) & (target_x < total_x), (target_y >= 0) & (target_y < total_y)], axis=-1
     )
-    minus_own = (couplings * (-reach.astype(jnp.float32))[:, :, :, None]).reshape(
-        (nx, ny, 2) + blk
-    )
+    minus_own = couplings.reshape((nx, ny, 2) + blk) * (-reach.astype(jnp.float32))[
+        :, :, :, None, None
+    ]
     factor_own = inv_factors.reshape((nx, ny) + blk)
     fine_own = (1 - coarse).astype(jnp.float32)[:, :, None, None] * left_gram(
         factor_own, factor_own

time: 82.6 us -> 82.4 us (level)
  the two profiles are of different devices: /device:TPU:121 before, /device:TPU:123 now
where the time goes in v2:
time: 82.4 us; the launch traced here: 81.8 us
  starting transfers between devices  29.8 us (36%)
  Pallas kernels  18.1 us (22%)
  local copies, waits for them, and re-layouts  15 us (18%)
  waiting for transfers between devices  13.3 us (16%)
  other arithmetic  3.31 us (4%)
  matrix products  1.4 us (2%)
  between operations  0.87 us (1%)
    ppermute x4, starting transfers between devices, on_device(): lax.ppermute(buffer, ('gx', 'gy'), corner_pairs(n_gx, n_gy, *step))  15.5 us
    pallas_call x1, Pallas kernels, local_compute(): pl.pallas_call(local_kernel, out_shape=(jax.ShapeDtypeStruct((nx * ny * 2...  14 us
    ppermute x1, waiting for transfers between devices, on_device(): from_yhi = lax.ppermute(packed[3], 'gy', shift_pairs(n_gy, -1))  5.6 us
    ppermute x1, waiting for transfers between devices, on_device(): from_xhi = lax.ppermute(packed[1], 'gx', shift_pairs(n_gx, -1))  5.59 us
    ppermute x1, starting transfers between devices, on_device(): from_xlo = lax.ppermute(packed[0], 'gx', shift_pairs(n_gx, 1))  5.31 us
    reshape x1, local copies, waits for them, and re-layouts, on_device(): return (strong, restrict.reshape(CAP, 14, flat))  5.02 us
    ppermute x1, starting transfers between devices, on_device(): from_ylo = lax.ppermute(packed[2], 'gy', shift_pairs(n_gy, 1))  5.01 us
    pallas_call x1, Pallas kernels, pack_buffers(): pl.pallas_call(pack_kernel, out_shape=tuple(shapes), in_specs=[smem, vmem...  4.13 us
  transfers between devices with their start and end apart: 8, of which 3 were waited for; matrix products, arithmetic and copies ran while one was open for 4% of the time, Pallas kernels for 0%

profile of v2, /device:TPU:123, one launch (start us, length us, event | category | flops | bytes accessed | tf_op | source)
XLA Modules:
  0.0 81.8 jit_solution(15491083136099783620)
XLA Ops:
  0.6 0.7 subtract_convert_fusion
  1.3 0.8 copy.51
  2.1 0.8 %compare_and_fusion.1 = (pred[4,4,1]{1,2,0:T(4,128)(4,1)S(1)}, pred[4,4,1]{1,2,0:T(4,128)(4,1)S(1)}) fusion(s32[4]{0:T(128)S(1)} %get-tuple-element.39, s32[4,4,2]{1,2,0:T(2,128)} %param.6, s32[4]{0:T(128)S(1)} %get-tuple-element.38), kind=kLoop, calls=%fused_computation.17 | loop fusion | flops 192 | bytes 192 | tf_op jit(solution)/shard_map/and | solution.py:303
  3.0 0.1 copy.53
  3.1 0.6 reshape.190.side_ref
  3.7 1.2 %reshape.191.factor_ref = f32[4,4,64,64]{3,2,1,0:T(8,128)S(1)} reshape(f32[4,4,4096]{2,1,0:T(4,128)} %param.4) | data formatting | bytes 524288 | tf_op jit(solution)/shard_map/reshape | solution.py:308
  4.9 1.9 %reshape.192 = f32[4,4,2,64,64]{4,3,2,1,0:T(8,128)S(1)} reshape(f32[4,4,2,4096]{3,2,1,0:T(2,128)} %param.5) | data formatting | bytes 1048576 | tf_op jit(solution)/shard_map/reshape | solution.py:305
  6.8 1.4 %convolution_multiply_fusion.fine_ref = f32[4,4,64,64]{3,2,1,0:T(8,128)} fusion(f32[4,4,64,64]{3,2,1,0:T(8,128)S(1)} %reshape.191.factor_ref, f32[4,4]{1,0:T(4,128)S(1)} %subtract_convert_fusion), kind=kOutput, calls=%fused_computation.1 | convolution fusion | flops 25231360 | bytes 524352 | tf_op jit(solution)/shard_map/...ji,...jk->...ik/dot_general | solution.py:15
  8.2 1.1 %broadcast_multiply_fusion.minus_ref = f32[4,4,2,64,64]{4,3,2,1,0:T(8,128)} fusion(f32[4,4,2,64,64]{4,3,2,1,0:T(8,128)S(1)} %reshape.192, f32[4,4,2]{2,1,0:T(4,128)S(1)} %copy.53), kind=kLoop, calls=%fused_computation.2 | loop fusion | flops 131072 | bytes 1048704 | tf_op jit(solution)/shard_map/mul | solution.py:305
  9.3 4.1 %shard_map.59 = (f32[4,4,2,64,64]{4,3,2,1,0:T(8,128)}, f32[17,64,128]{2,1,0:T(8,128)}, f32[17,64,128]{2,1,0:T(8,128)}, f32[17,64,128]{2,1,0:T(8,128)}, f32[17,64...) custom-call(s32[32]{0:T(128)} %reshape.190.side_ref, ...), custom_call_target="tpu_custom_call" | custom-call | tf_op jit(solution)/shard_map/pallas_call | solution.py:258
  13.4 5.9 %collective-permute-start = (f32[4,64,128]{2,1,0:T(8,128)}, f32[4,64,128]{2,1,0:T(8,128)S(1)}, u32[]{:S(2)}, u32[]{:S(2)}) collective-permute-start(f32[4,64,128]{2,1,0:T(8,128)} %get-tuple-element.13), channel_id=1, source_target_pairs={{0,17},{1,18},{2,19},{3,20},{4,21},{5,22},{6,23},{7,24},{8,25},{9,... | collective-permute-start | bytes 393224 | tf_op jit(solution)/shard_map/ppermute | solution.py:320
  19.3 1.9 %collective-permute-start.2 = (f32[4,64,128]{2,1,0:T(8,128)}, f32[4,64,128]{2,1,0:T(8,128)S(1)}, u32[]{:S(2)}, u32[]{:S(2)}) collective-permute-start(f32[4,64,128]{2,1,0:T(8,128)} %get-tuple-element.15), channel_id=1, source_target_pairs={{1,16},{2,17},{3,18},{4,19},{5,20},{6,21},{7,22},{8,23},{9,24},{10... | collective-permute-start | bytes 393224 | tf_op jit(solution)/shard_map/ppermute | solution.py:320
  21.3 5.8 %collective-permute-start.5 = (f32[4,64,128]{2,1,0:T(8,128)}, f32[4,64,128]{2,1,0:T(8,128)S(1)}, u32[]{:S(2)}, u32[]{:S(2)}) collective-permute-start(f32[4,64,128]{2,1,0:T(8,128)} %get-tuple-element.18), channel_id=1, source_target_pairs={{16,1},{17,2},{18,3},{19,4},{20,5},{21,6},{22,7},{23,8},{24,9},{25... | collective-permute-start | bytes 393224 | tf_op jit(solution)/shard_map/ppermute | solution.py:320
  27.0 1.9 %collective-permute-start.7 = (f32[4,64,128]{2,1,0:T(8,128)}, f32[4,64,128]{2,1,0:T(8,128)S(1)}, u32[]{:S(2)}, u32[]{:S(2)}) collective-permute-start(f32[4,64,128]{2,1,0:T(8,128)} %get-tuple-element.20), channel_id=1, source_target_pairs={{17,0},{18,1},{19,2},{20,3},{21,4},{22,5},{23,6},{24,7},{25,8},{26... | collective-permute-start | bytes 393224 | tf_op jit(solution)/shard_map/ppermute | solution.py:320
  29.0 5.3 %collective-permute-start.1 = (f32[17,64,128]{2,1,0:T(8,128)}, f32[17,64,128]{2,1,0:T(8,128)S(1)}, u32[]{:S(2)}, u32[]{:S(2)}) collective-permute-start(f32[17,64,128]{2,1,0:T(8,128)} %get-tuple-element.14), channel_id=1, source_target_pairs={{0,16},{16,32},{32,48},{48,64},{64,80},{80,96},{96,112},{112,128},... | collective-permute-start | bytes 1671176 | tf_op jit(solution)/shard_map/ppermute | solution.py:314
  34.3 0.0 copy-done.10
  34.3 0.1 reshape.196
  34.4 0.1 reshape.208
  34.5 0.0 copy-done.9
  34.5 0.1 add_reduce_fusion.1
  34.6 0.1 stack.15
  34.6 0.1 stack.16
  34.8 0.1 reduce.4
  34.9 0.1 select_reduce_fusion
  35.0 0.1 copy.64
  35.1 0.1 copy.66
  35.2 0.1 copy.65
  35.3 0.6 gather_fusion
  35.9 0.1 pad_add_fusion.4
  35.9 0.7 reshape.197.slot_ref
  36.6 0.0 collective-permute-done.cll_ref
  36.6 5.0 %collective-permute-start.3 = (f32[17,64,128]{2,1,0:T(8,128)}, f32[17,64,128]{2,1,0:T(8,128)S(1)}, u32[]{:S(2)}, u32[]{:S(2)}) collective-permute-start(f32[17,64,128]{2,1,0:T(8,128)} %get-tuple-element.16), channel_id=1, source_target_pairs={{0,1},{1,2},{2,3},{3,4},{4,5},{5,6},{6,7},{7,8},{8,9},{9,10},{10,1... | collective-permute-start | bytes 1671176 | tf_op jit(solution)/shard_map/ppermute | solution.py:316
  41.6 0.0 collective-permute-done.2.clh_ref
  41.7 1.9 %collective-permute-start.4 = (f32[17,64,128]{2,1,0:T(8,128)}, f32[17,64,128]{2,1,0:T(8,128)S(1)}, u32[]{:S(2)}, u32[]{:S(2)}) collective-permute-start(f32[17,64,128]{2,1,0:T(8,128)} %get-tuple-element.17), channel_id=1, source_target_pairs={{1,0},{2,1},{3,2},{4,3},{5,4},{6,5},{7,6},{8,7},{9,8},{10,9},{11,1... | collective-permute-start | bytes 1671176 | tf_op jit(solution)/shard_map/ppermute | solution.py:317
  43.6 0.0 collective-permute-done.5.chl_ref
  43.6 2.1 %collective-permute-start.6 = (f32[17,64,128]{2,1,0:T(8,128)}, f32[17,64,128]{2,1,0:T(8,128)S(1)}, u32[]{:S(2)}, u32[]{:S(2)}) collective-permute-start(f32[17,64,128]{2,1,0:T(8,128)} %get-tuple-element.19), channel_id=1, source_target_pairs={{16,0},{32,16},{48,32},{64,48},{80,64},{96,80},{112,96},{128,112},... | collective-permute-start | bytes 1671176 | tf_op jit(solution)/shard_map/ppermute | solution.py:315
  45.7 0.1 copy.69
  45.8 0.1 copy.70
  45.9 0.1 copy.71
  46.0 0.0 collective-permute-done.7.chh_ref
  46.0 0.1 copy.72
  46.1 0.0 collective-permute-done.1.xlo_ref
  46.1 0.1 convert_element_type.61
  46.2 0.1 copy.55
  46.3 2.1 %collective-permute-done.3.ylo_ref = f32[17,64,128]{2,1,0:T(8,128)S(1)} collective-permute-done((f32[17,64,128]{2,1,0:T(8,128)}, f32[17,64,128]{2,1,0:T(8,128)S(1)}, u32[]{:S(2)}, u32[]{:S(2)}) %collective-permute-start.3) | collective-permute-done | bytes 557088 | tf_op jit(solution)/shard_map/ppermute | solution.py:316
  48.4 0.1 convert_element_type.64
  48.5 0.1 copy.57
  48.6 5.6 %collective-permute-done.4.yhi_ref = f32[17,64,128]{2,1,0:T(8,128)S(1)} collective-permute-done((f32[17,64,128]{2,1,0:T(8,128)}, f32[17,64,128]{2,1,0:T(8,128)S(1)}, u32[]{:S(2)}, u32[]{:S(2)}) %collective-permute-start.4) | collective-permute-done | bytes 557088 | tf_op jit(solution)/shard_map/ppermute | solution.py:317
  54.2 0.1 convert_element_type.66
  54.3 0.1 copy.58
  54.4 5.6 %collective-permute-done.6.xhi_ref = f32[17,64,128]{2,1,0:T(8,128)S(1)} collective-permute-done((f32[17,64,128]{2,1,0:T(8,128)}, f32[17,64,128]{2,1,0:T(8,128)S(1)}, u32[]{:S(2)}, u32[]{:S(2)}) %collective-permute-start.6) | collective-permute-done | bytes 557088 | tf_op jit(solution)/shard_map/ppermute | solution.py:315
  60.1 0.1 convert_element_type.69
  60.1 0.1 copy.60
  60.3 0.1 fusion
  60.3 0.1 copy.62
  60.5 0.7 reshape.193.side_ref
  61.1 0.0 copy-done.5
  61.1 0.0 copy-done.1
  61.1 0.0 copy-done.2
  61.2 14.0 %shard_map.60 = (f32[32,128]{1,0:T(8,128)}, bf16[12,14,64,64]{3,2,1,0:T(8,128)(2,1)}) custom-call(s32[128]{0:T(128)} %reshape.193.side_ref, s32[48]{0:T(128)} %reshape.197.slot_ref, f32[4,4,64,64]{3,2,1,0:T(8,128)} %convolution_multiply_fusion.fine_ref, f32[4,4,2,64,64]{4,3,2,1,0:T(8,128)} %get-tuple-element.21.lead_ref, f32[4,4,64,64]{3,2,1,0:T(8,128)} %copy-done, ...), custom_call_target="tpu_custom_call" | custom-call | tf_op jit(solution)/shard_map/pallas_call | solution.py:272
  75.1 0.8 %slice_reduce_fusion = f32[32]{0:T(128)S(1)} fusion(f32[32,128]{1,0:T(8,128)} %get-tuple-element.22), kind=kLoop, calls=%fused_computation.3 | loop fusion | bytes 256 | tf_op jit(solution)/shard_map/slice | solution.py:287
  76.0 0.1 reshape_squeeze.3
  76.1 0.7 copy.67
  76.8 5.0 %reshape.198 = bf16[12,14,4096]{2,1,0:T(8,128)(2,1)} reshape(bf16[12,14,64,64]{3,2,1,0:T(8,128)(2,1)} %get-tuple-element.23) | data formatting | bytes 2752512 | tf_op jit(solution)/shard_map/reshape | solution.py:379
  (33 shorter events, 0.2 us)
Async XLA Ops:
  4.9 4.4 %copy-start = (f32[4,4,64,64]{3,2,1,0:T(8,128)}, f32[4,4,64,64]{3,2,1,0:T(8,128)S(1)}, u32[]{:S(2)}) copy-start(f32[4,4,64,64]{3,2,1,0:T(8,128)S(1)} %reshape.191.factor_ref) | copy-start | bytes 786436
  6.8 27.5 %copy-start.10 = (s32[4,4]{1,0:T(4,128)S(1)}, s32[4,4]{1,0:T(4,128)}, u32[]{:S(2)}) copy-start(s32[4,4]{1,0:T(4,128)} %param.7) | copy-start | bytes 196
  6.8 27.7 %copy-start.9 = (s32[4,4,2]{1,2,0:T(2,128)S(1)}, s32[4,4,2]{1,2,0:T(2,128)}, u32[]{:S(2)}) copy-start(s32[4,4,2]{1,2,0:T(2,128)} %param.6) | copy-start | bytes 388
  13.4 23.2 %collective-permute-start = (f32[4,64,128]{2,1,0:T(8,128)}, f32[4,64,128]{2,1,0:T(8,128)S(1)}, u32[]{:S(2)}, u32[]{:S(2)}) collective-permute-start(f32[4,64,128]{2,1,0:T(8,128)} %get-tuple-element.13), channel_id=1, source_target_pairs={{0,17},{1,18},{2,19},{3,20},{4,21},{5,22},{6,23},{7,24},{8,25},{9,... | collective-permute-start | bytes 393224 | tf_op jit(solution)/shard_map/ppermute | solution.py:320
  19.3 22.3 %collective-permute-start.2 = (f32[4,64,128]{2,1,0:T(8,128)}, f32[4,64,128]{2,1,0:T(8,128)S(1)}, u32[]{:S(2)}, u32[]{:S(2)}) collective-permute-start(f32[4,64,128]{2,1,0:T(8,128)} %get-tuple-element.15), channel_id=1, source_target_pairs={{1,16},{2,17},{3,18},{4,19},{5,20},{6,21},{7,22},{8,23},{9,24},{10... | collective-permute-start | bytes 393224 | tf_op jit(solution)/shard_map/ppermute | solution.py:320
  21.3 22.3 %collective-permute-start.5 = (f32[4,64,128]{2,1,0:T(8,128)}, f32[4,64,128]{2,1,0:T(8,128)S(1)}, u32[]{:S(2)}, u32[]{:S(2)}) collective-permute-start(f32[4,64,128]{2,1,0:T(8,128)} %get-tuple-element.18), channel_id=1, source_target_pairs={{16,1},{17,2},{18,3},{19,4},{20,5},{21,6},{22,7},{23,8},{24,9},{25... | collective-permute-start | bytes 393224 | tf_op jit(solution)/shard_map/ppermute | solution.py:320
  27.0 19.0 %collective-permute-start.7 = (f32[4,64,128]{2,1,0:T(8,128)}, f32[4,64,128]{2,1,0:T(8,128)S(1)}, u32[]{:S(2)}, u32[]{:S(2)}) collective-permute-start(f32[4,64,128]{2,1,0:T(8,128)} %get-tuple-element.20), channel_id=1, source_target_pairs={{17,0},{18,1},{19,2},{20,3},{21,4},{22,5},{23,6},{24,7},{25,8},{26... | collective-permute-start | bytes 393224 | tf_op jit(solution)/shard_map/ppermute | solution.py:320
  29.0 17.2 %collective-permute-start.1 = (f32[17,64,128]{2,1,0:T(8,128)}, f32[17,64,128]{2,1,0:T(8,128)S(1)}, u32[]{:S(2)}, u32[]{:S(2)}) collective-permute-start(f32[17,64,128]{2,1,0:T(8,128)} %get-tuple-element.14), channel_id=1, source_target_pairs={{0,16},{16,32},{32,48},{48,64},{64,80},{80,96},{96,112},{112,128},... | collective-permute-start | bytes 1671176 | tf_op jit(solution)/shard_map/ppermute | solution.py:314
  36.6 24.5 %copy-start.5 = (f32[4,64,128]{2,1,0:T(8,128)}, f32[4,64,128]{2,1,0:T(8,128)S(1)}, u32[]{:S(2)}) copy-start(f32[4,64,128]{2,1,0:T(8,128)S(1)} %collective-permute-done.cll_ref) | copy-start | bytes 393220
  36.6 11.8 %collective-permute-start.3 = (f32[17,64,128]{2,1,0:T(8,128)}, f32[17,64,128]{2,1,0:T(8,128)S(1)}, u32[]{:S(2)}, u32[]{:S(2)}) collective-permute-start(f32[17,64,128]{2,1,0:T(8,128)} %get-tuple-element.16), channel_id=1, source_target_pairs={{0,1},{1,2},{2,3},{3,4},{4,5},{5,6},{6,7},{7,8},{8,9},{9,10},{10,1... | collective-permute-start | bytes 1671176 | tf_op jit(solution)/shard_map/ppermute | solution.py:316
  41.6 19.5 %copy-start.6 = (f32[4,64,128]{2,1,0:T(8,128)}, f32[4,64,128]{2,1,0:T(8,128)S(1)}, u32[]{:S(2)}) copy-start(f32[4,64,128]{2,1,0:T(8,128)S(1)} %collective-permute-done.2.clh_ref) | copy-start | bytes 393220
  41.7 12.6 %collective-permute-start.4 = (f32[17,64,128]{2,1,0:T(8,128)}, f32[17,64,128]{2,1,0:T(8,128)S(1)}, u32[]{:S(2)}, u32[]{:S(2)}) collective-permute-start(f32[17,64,128]{2,1,0:T(8,128)} %get-tuple-element.17), channel_id=1, source_target_pairs={{1,0},{2,1},{3,2},{4,3},{5,4},{6,5},{7,6},{8,7},{9,8},{10,9},{11,1... | collective-permute-start | bytes 1671176 | tf_op jit(solution)/shard_map/ppermute | solution.py:317
  43.6 17.5 %copy-start.7 = (f32[4,64,128]{2,1,0:T(8,128)}, f32[4,64,128]{2,1,0:T(8,128)S(1)}, u32[]{:S(2)}) copy-start(f32[4,64,128]{2,1,0:T(8,128)S(1)} %collective-permute-done.5.chl_ref) | copy-start | bytes 393220
  43.6 16.4 %collective-permute-start.6 = (f32[17,64,128]{2,1,0:T(8,128)}, f32[17,64,128]{2,1,0:T(8,128)S(1)}, u32[]{:S(2)}, u32[]{:S(2)}) collective-permute-start(f32[17,64,128]{2,1,0:T(8,128)} %get-tuple-element.19), channel_id=1, source_target_pairs={{16,0},{32,16},{48,32},{64,48},{80,64},{96,80},{112,96},{128,112},... | collective-permute-start | bytes 1671176 | tf_op jit(solution)/shard_map/ppermute | solution.py:315
  46.0 15.1 %copy-start.8 = (f32[4,64,128]{2,1,0:T(8,128)}, f32[4,64,128]{2,1,0:T(8,128)S(1)}, u32[]{:S(2)}) copy-start(f32[4,64,128]{2,1,0:T(8,128)S(1)} %collective-permute-done.7.chh_ref) | copy-start | bytes 393220
  46.1 15.0 %copy-start.1 = (f32[17,64,128]{2,1,0:T(8,128)}, f32[17,64,128]{2,1,0:T(8,128)S(1)}, u32[]{:S(2)}) copy-start(f32[17,64,128]{2,1,0:T(8,128)S(1)} %collective-permute-done.1.xlo_ref) | copy-start | bytes 1671172
  48.4 12.8 %copy-start.2 = (f32[17,64,128]{2,1,0:T(8,128)}, f32[17,64,128]{2,1,0:T(8,128)S(1)}, u32[]{:S(2)}) copy-start(f32[17,64,128]{2,1,0:T(8,128)S(1)} %collective-permute-done.3.ylo_ref) | copy-start | bytes 1671172
  54.2 6.9 %copy-start.3 = (f32[17,64,128]{2,1,0:T(8,128)}, f32[17,64,128]{2,1,0:T(8,128)S(1)}, u32[]{:S(2)}) copy-start(f32[17,64,128]{2,1,0:T(8,128)S(1)} %collective-permute-done.4.yhi_ref) | copy-start | bytes 1671172
  60.0 1.1 %copy-start.4 = (f32[17,64,128]{2,1,0:T(8,128)}, f32[17,64,128]{2,1,0:T(8,128)S(1)}, u32[]{:S(2)}) copy-start(f32[17,64,128]{2,1,0:T(8,128)S(1)} %collective-permute-done.6.xhi_ref) | copy-start | bytes 1671172
